TPU v7x, 256 devices: a whole 4x4x8 slice. The times are simulated.
256 devices in a mesh: row: 64 (over x, z_hi, y), col: 4 (over z_lo, core).
Axes of the slice: x: 4, y: 4, z: 8 (z_hi: 4, z_lo: 2; z = z_hi * 2 + z_lo), core: 2. Of those that a mesh axis runs over, the one named last changes fastest.
Arguments:
- img_hidden: bfloat16 [8, 1536, 2432], P(None, 'row', 'col'), may hold values from -6 to 6
- txt_hidden: bfloat16 [8, 128, 2432], P(None, 'row', 'col'), may hold values from -6 to 6
- latent: float32 [8, 1536, 64], P(None, 'row'), may hold values from -6 to 6
- img_mod: float32 [8, 5, 2432], replicated, may hold values from -4 to 4
- txt_mod: float32 [8, 2, 2432], replicated, may hold values from -4 to 4
- qkv_weight: bfloat16 [3, 2432, 2048], P(None, None, 'col'), may hold values from -0.125 to 0.125
- txt_kv_weight: bfloat16 [2, 2432, 2048], P(None, None, 'col'), may hold values from -0.125 to 0.125
- out_weight: bfloat16 [2048, 2432], P('col', 'row'), may hold values from -0.125 to 0.125
- final_weight: bfloat16 [2432, 64], P('col'), may hold values from -0.125 to 0.125
- qk_gains: float32 [3, 64], replicated, may hold values from 1.5 to 9
- txt_len: int32 [8], replicated, may hold values from 1 to 128, as said below
- step_idx: int32 [8], replicated, may hold values from 1 to 28
Outputs:
- advanced: float32 [8, 1536, 64], P(None, 'row')
- denoised: float32 [8, 1536, 64], P(None, 'row')
Inputs may be any that keep to these rules, and one draw needn't show every extreme that they name: `txt_len`: some request has all 128 text tokens live.
All inputs are finite; a program needn't handle non-finite values.
Results may differ from a plain program's by a relative error of at most 0.0044.
The roundings to bfloat16 on the way count: a program that leaves them out, or rounds other values in their place, can miss the bound.
Values may be sent and summed in bfloat16 or wider, within the bound.
No kernel may reach another device: no remote copies, remote signals or barrier semaphores. Data moves between devices by JAX's collectives and lax.ppermute only.
A program may use at most 128 MiB of HBM per device.

v0:
```python
import jax
import jax.numpy as jnp
from jax import lax
from jax.sharding import Mesh
from jax.sharding import PartitionSpec as P

D = 2432
HD = 64
STEPS = 28
REQ = 8
ROW = ("rq", "rm")
eps_norm = 1e-06
neg_fill = -1e30


def layer_norm(values):
    average = jnp.mean(values, -1, keepdims=True)
    centred = values - average
    variance = jnp.mean(centred * centred, -1, keepdims=True)
    return centred * lax.rsqrt(variance + eps_norm)


def rms_heads(values, scaling):
    reshaped = values.reshape(values.shape[:-1] + (values.shape[-1] // HD, HD))
    inverse = lax.rsqrt(jnp.mean(reshaped * reshaped, -1, keepdims=True) + eps_norm)
    return (reshaped * inverse * scaling).astype(jnp.bfloat16)


def sigma_at(indices):
    fraction = indices.astype(jnp.float32) / STEPS
    return 3.0 * fraction / (1.0 + 2.0 * fraction)


def gather_features(local):
    stacked = lax.all_gather(local, "col", axis=0, tiled=False)
    slabs = stacked.shape[0]
    moved = jnp.moveaxis(stacked, 0, -2)
    return moved.reshape(local.shape[:-1] + (slabs * local.shape[-1],))


def attend_one(queries, keys, values, allowed):
    scores = jnp.einsum("qhd,khd->hqk", queries, keys, preferred_element_type=jnp.float32) * HD ** (
        -0.5
    )
    scores = jnp.where(allowed[None, None, :], scores, neg_fill)
    top_score = jnp.max(scores, -1, keepdims=True)
    exp_scores = jnp.where(allowed[None, None, :], jnp.exp(scores - top_score), 0.0)
    row_total = jnp.sum(exp_scores, -1)
    weighted = jnp.einsum(
        "hqk,khd->qhd", exp_scores.astype(jnp.bfloat16), values, preferred_element_type=jnp.float32
    )
    return (weighted / jnp.transpose(row_total)[..., None]).astype(jnp.bfloat16)


def per_device(
    img_hidden,
    txt_hidden,
    latent,
    img_mod,
    txt_mod,
    qkv_weight,
    txt_kv_weight,
    out_weight,
    final_weight,
    qk_gains,
    txt_len,
    step_idx,
):
    requests = img_hidden.shape[0]
    patches = img_hidden.shape[1]
    text_rows = txt_hidden.shape[1]
    cols_local = qkv_weight.shape[2]
    heads_local = cols_local // HD
    block_len = patches + text_rows
    groups = lax.axis_size("rq")
    members = lax.axis_size("rm")
    weight_t = lax.all_gather(jnp.transpose(out_weight), ROW, axis=0, tiled=True)
    img_full = gather_features(img_hidden)
    txt_full = gather_features(txt_hidden)
    img_wide = img_full.astype(jnp.float32)
    normed = (layer_norm(img_wide) * (1.0 + img_mod[:, 1:2, :]) + img_mod[:, 0:1, :]).astype(
        jnp.bfloat16
    )
    flat_rows = normed.reshape(requests * patches, D)
    projected = jnp.einsum("td,cde->cte", flat_rows, qkv_weight, preferred_element_type=jnp.float32)
    queries = rms_heads(projected[0], qk_gains[0]).reshape(requests, patches, cols_local)
    img_keys = rms_heads(projected[1], qk_gains[1]).reshape(requests, patches, cols_local)
    img_values = projected[2].astype(jnp.bfloat16).reshape(requests, patches, cols_local)
    text_normed = (
        layer_norm(txt_full.astype(jnp.float32)) * (1.0 + txt_mod[:, 1:2, :]) + txt_mod[:, 0:1, :]
    ).astype(jnp.bfloat16)
    text_proj = jnp.einsum(
        "rtd,cde->crte", text_normed, txt_kv_weight, preferred_element_type=jnp.float32
    )
    text_keys = rms_heads(text_proj[0], qk_gains[2]).reshape(requests, text_rows, cols_local)
    text_values = text_proj[1].astype(jnp.bfloat16)
    key_rows = jnp.concatenate([img_keys, text_keys], 1)
    value_rows = jnp.concatenate([img_values, text_values], 1)
    kv_rows = jnp.stack([key_rows, value_rows], 1)
    group_queries = lax.all_to_all(queries, "rq", 0, 0, tiled=True)
    group_kv = lax.all_to_all(kv_rows, "rq", 0, 0, tiled=True)
    all_kv = lax.all_gather(group_kv, "rm", axis=0, tiled=False)
    key_count = members * groups * block_len
    keys = all_kv[:, :, 0].reshape(key_count, heads_local, HD)
    values = all_kv[:, :, 1].reshape(key_count, heads_local, HD)
    request = lax.axis_index("rq")
    positions = jnp.arange(key_count, dtype=jnp.int32)
    within = positions % block_len
    source_block = positions // block_len
    member_of = source_block // groups
    group_of = source_block % groups
    source_row = group_of * members + member_of
    text_pos = source_row * text_rows + within - patches
    live_text = text_pos < lax.dynamic_index_in_dim(txt_len, request, keepdims=False)
    allowed = (within < patches) | live_text
    attended = attend_one(
        group_queries.reshape(groups * patches, heads_local, HD), keys, values, allowed
    ).reshape(groups, patches, cols_local)
    attended = lax.all_to_all(attended, "rq", 0, 0, tiled=True).reshape(
        requests * patches, cols_local
    )
    partial_value = lax.dot_general(
        attended, weight_t, (((1,), (1,)), ((), ())), preferred_element_type=jnp.float32
    )
    slab_width = img_hidden.shape[2]
    col_index = lax.axis_index("col")
    shared_sum = lax.psum_scatter(partial_value, "col", scatter_dimension=1, tiled=True)
    col_mods = lax.dynamic_slice_in_dim(img_mod, col_index * slab_width, slab_width, 2)
    mixed = img_hidden.astype(jnp.float32) + col_mods[:, 2:3, :] * shared_sum.reshape(
        requests, patches, slab_width
    )
    row_sums, squares = lax.psum((jnp.sum(mixed, -1), jnp.sum(mixed * mixed, -1)), "col")
    row_mean = row_sums / D
    spread = squares / D - row_mean * row_mean
    scaled = (mixed - row_mean[..., None]) * lax.rsqrt(spread[..., None] + eps_norm)
    modulated = (scaled * (1.0 + col_mods[:, 4:5, :]) + col_mods[:, 3:4, :]).astype(jnp.bfloat16)
    velocity = lax.psum(
        jnp.dot(
            modulated.reshape(requests * patches, slab_width),
            final_weight,
            preferred_element_type=jnp.float32,
        ),
        "col",
    )
    velocity = velocity.reshape(requests, patches, latent.shape[2])
    sigma_now = sigma_at(step_idx)[:, None, None]
    sigma_next = sigma_at(step_idx - 1)[:, None, None]
    advanced = latent + (sigma_next - sigma_now) * velocity
    denoised = latent - sigma_now * velocity
    return (advanced, denoised)


def solution(mesh):
    rows = mesh.shape["row"]
    cols = mesh.shape["col"]
    split = Mesh(mesh.devices.reshape(REQ, rows // REQ, cols), ("rq", "rm", "col"))
    in_specs = (
        P(None, ROW, "col"),
        P(None, ROW, "col"),
        P(None, ROW, None),
        P(),
        P(),
        P(None, None, "col"),
        P(None, None, "col"),
        P("col", ROW),
        P("col", None),
        P(),
        P(),
        P(),
    )
    out_specs = (P(None, ROW, None), P(None, ROW, None))
    return jax.shard_map(
        per_device, mesh=split, in_specs=in_specs, out_specs=out_specs, check_vma=False
    )
```

profile of v0, /device:TPU:1, one launch (start us, length us, event | category | flops | bytes accessed | tf_op | source)
XLA Modules:
  0.0 299.0 jit_solution(12010077146269406684)
XLA Ops:
  7.2 8.6 %all-gather.1 = bf16[32,2,608]{2,1,0:T(2,128)(2,1)S(1)} all-gather(bf16[8,2,608]{2,1,0:T(2,128)(2,1)} %param.13), channel_id=3, replica_groups=mesh['rq'=8,'rm'=8,'col'=4] {'col'}, dimensions={0}, use_global_device_ids=true | all-gather | bytes 97280 | tf_op jit(solution)/shard_map/all_gather | solution.py:35
  16.1 10.0 %all-gather = bf16[32,24,608]{2,1,0:T(8,128)(2,1)S(1)} all-gather(bf16[8,24,608]{2,1,0:T(8,128)(2,1)} %param.12), channel_id=2, replica_groups=mesh['rq'=8,'rm'=8,'col'=4] {'col'}, dimensions={0}, use_global_device_ids=true | all-gather | bytes 1167360 | tf_op jit(solution)/shard_map/all_gather | solution.py:35
  27.9 3.2 %fusion.28 = f32[2,8,2,512]{3,1,0,2:T(8,128)S(1)} fusion(bf16[2,2432,512]{2,1,0:T(8,128)(2,1)} %param.18, f32[8,2,2432]{2,0,1:T(8,128)S(1)} %reshape.182, f32[8,2432]{1,0:T(8,128)S(1)} %get-tuple-element.30, f32[8,2432]{1,0:T(8,128)S(1)} %get-tuple-element.31, f32[8,2]{0,1:T(2,128)S(1)} %copy.88, f32[8,2]{0,1:T(2,128)S(1)} %copy.85), kind=kOutput, calls=%fused_computation.26 | convolution fusion | flops 79886336 | bytes 5357696 | tf_op jit(solution)/shard_map/rtd,cde->crte/dot_general | solution.py:92
  31.2 2.6 copy.80
  33.8 2.2 reshape.181
  36.0 0.9 add_bitcast_fusion
  37.5 4.8 %convolution_bitcast_fusion.1 = f32[3,192,512]{2,1,0:T(8,128)S(1)} fusion(bf16[3,2432,512]{2,1,0:T(8,128)(2,1)} %param.17, bf16[192,2432]{1,0:T(8,128)(2,1)S(1)} %fusion.12), kind=kOutput, calls=%fused_computation.22 | convolution fusion | flops 1434451968 | bytes 9584640 | tf_op jit(solution)/shard_map/td,cde->cte/dot_general | solution.py:85
  44.6 21.4 %all_to_all.15 = bf16[8,2,26,512]{3,1,2,0:T(2,128)(2,1)} all-to-all(bf16[8,2,26,512]{3,1,2,0:T(2,128)(2,1)S(1)} %copy.93), channel_id=1, replica_groups=mesh['rq'=8,'rm'=8,'col'=4] {'rq'}, dimensions={0} | all-to-all | bytes 851968 | tf_op jit(solution)/shard_map/all_to_all | solution.py:101
  66.2 0.7 all-gather.9.cloned.1.call-update
  67.8 0.7 multiply_convert_fusion
  68.6 3.6 %all-to-all-start.1 = ((bf16[8,24,512]{2,1,0:T(8,128)(2,1)}), bf16[8,24,512]{2,1,0:T(8,128)(2,1)S(1)}, u32[]{:S(2)}, u32[]{:S(2)}) async-start(bf16[8,24,512]{2,1,0:T(8,128)(2,1)} %multiply_convert_fusion), calls=%async_computation.1 | async-start | bytes 393216 | tf_op jit(solution)/shard_map/all_to_all | solution.py:100
  72.7 0.7 fusion.60
  73.4 8.2 %all-to-all-done.1 = bf16[8,24,512]{2,1,0:T(8,128)(2,1)S(1)} async-done(((bf16[8,24,512]{2,1,0:T(8,128)(2,1)}), bf16[8,24,512]{2,1,0:T(8,128)(2,1)S(1)}, u32[]{:S(2)}, u32[]{:S(2)}) %all-to-all-start.1) | async-done | bytes 196640 | tf_op jit(solution)/shard_map/all_to_all | solution.py:100
  81.6 1.0 reshape.175
  82.6 66.5 %all-gather.7.cloned.1.call-done = bf16[64,2,26,512]{3,1,2,0:T(2,128)(2,1)} async-done(((bf16[8,2,26,512]{3,1,2,0:T(2,128)(2,1)}), bf16[64,2,26,512]{3,1,2,0:T(2,128)(2,1)}) %all-gather.7.cloned.1.call-update) | async-done | bytes 3407888 | tf_op jit(solution)/shard_map/all_gather | solution.py:102
  149.1 25.3 %slice_reduce_fusion.1 = (bf16[8,8,26,512]{3,2,1,0:T(8,128)(2,1)}, bf16[8,8,26,512]{3,2,1,0:T(8,128)(2,1)}) fusion(bf16[8,8,2,26,512]{4,2,3,1,0:T(2,128)(2,1)} %bitcast.118), kind=kLoop, calls=%fused_computation.13 | loop fusion | bytes 6815744 | tf_op jit(solution)/shard_map/slice | solution.py:105
  174.5 4.3 %reshape_squeeze.19 = bf16[1664,8,64]{2,1,0:T(8,128)(2,1)S(1)} reshape(bf16[8,8,26,512]{3,2,1,0:T(8,128)(2,1)} %get-tuple-element.3) | data formatting | bytes 3407872 | tf_op jit(solution)/shard_map/reshape;squeeze | solution.py:104
  178.8 5.7 %reshape_squeeze.17 = bf16[1664,8,64]{2,1,0:T(8,128)(2,1)} reshape(bf16[8,8,26,512]{3,2,1,0:T(8,128)(2,1)} %get-tuple-element.2) | data formatting | bytes 3407872 | tf_op jit(solution)/shard_map/reshape;squeeze | solution.py:105
  184.4 6.4 %fusion.10 = f32[8,192,1664]{2,1,0:T(8,128)} fusion(bf16[1664,8,64]{2,1,0:T(8,128)(2,1)S(1)} %reshape_squeeze.19, bf16[192,8,64]{2,1,0:T(8,128)(2,1)} %reshape.175), kind=kOutput, calls=%fused_computation.15 | convolution fusion | flops 327155712 | bytes 12124160 | tf_op jit(solution)/shard_map/qhd,khd->hqk/dot_general | solution.py:42
  190.9 12.9 %fusion.67 = (f32[8,192]{1,0:T(8,128)S(1)}, bf16[8,192,1664]{2,1,0:T(8,128)(2,1)}) fusion(f32[8,192,1664]{2,1,0:T(8,128)} %fusion.10, pred[1664]{0:T(1024)(128)(4,1)S(1)} %fusion.60), kind=kOutput, calls=%fused_computation.113 | output fusion | flops 20448896 | bytes 15343232 | tf_op jit(solution)/shard_map/sub | solution.py:47
  203.8 4.4 %fusion.23 = bf16[192,8,64]{0,2,1:T(8,128)(2,1)S(1)} fusion(bf16[8,192,1664]{2,1,0:T(8,128)(2,1)} %get-tuple-element.29, bf16[1664,8,64]{2,1,0:T(8,128)(2,1)S(1)} %copy-done.1, f32[192,8]{0,1:T(8,128)S(1)} %bitcast.132), kind=kOutput, calls=%fused_computation.25 | convolution fusion | flops 327352320 | bytes 7018496 | tf_op jit(solution)/shard_map/hqk,khd->qhd/dot_general | solution.py:49
  208.5 0.9 reshape.176
  209.4 7.7 %all-to-all-start.2 = ((bf16[8,24,512]{2,1,0:T(8,128)(2,1)}), bf16[8,24,512]{2,1,0:T(8,128)(2,1)S(1)}, u32[]{:S(2)}, u32[]{:S(2)}) async-start(bf16[8,24,512]{2,1,0:T(8,128)(2,1)} %reshape.176), calls=%async_computation.2 | async-start | bytes 393216 | tf_op jit(solution)/shard_map/all_to_all | solution.py:119
  217.1 15.6 %all-gather.9.cloned.1.call-done = bf16[64,38,512]{2,1,0:T(8,128)(2,1)} async-done(((bf16[1,38,512]{2,1,0:T(8,128)(2,1)}), bf16[64,38,512]{2,1,0:T(8,128)(2,1)}) %all-gather.9.cloned.1.call-update) | async-done | bytes 2490384 | tf_op jit(solution)/shard_map/all_gather | solution.py:77
  232.7 2.8 reshape.191
  235.5 2.3 convolution_bitcast_fusion
  237.8 0.9 dynamic-slice_bitcast_fusion.1
  238.7 34.1 %reduce-scatter.4.cloned.1.call-done = f32[608,192]{1,0:T(8,128)} async-done(((f32[2432,192]{1,0:T(8,128)}), f32[608,192]{1,0:T(8,128)}) %reduce-scatter.4.cloned.1.call-update) | async-done | bytes 466960
  272.9 1.3 copy.106
  274.3 5.5 %all-reduce = (f32[8,24]{1,0:T(8,128)S(1)}, f32[8,24]{1,0:T(8,128)S(1)}) all-reduce(f32[8,24]{1,0:T(8,128)S(1)} %get-tuple-element.5, f32[8,24]{1,0:T(8,128)S(1)} %get-tuple-element.4), channel_id=1, replica_groups=mesh['rq'=8,'rm'=8,'col'=4] {'col'}, use_global_device_ids=true, to_apply=%region_13.14 | all-reduce | flops 384 | bytes 3072 | tf_op jit(solution)/shard_map/psum | solution.py:132
  280.3 11.4 %psum.23 = f32[8,24,64]{2,1,0:T(8,128)S(1)} all-reduce(f32[8,24,64]{2,1,0:T(8,128)S(1)} %bitcast.130), channel_id=1, replica_groups=mesh['rq'=8,'rm'=8,'col'=4] {'col'}, use_global_device_ids=true, to_apply=%region_14.15 | all-reduce | flops 12288 | bytes 98304 | tf_op jit(solution)/shard_map/psum | solution.py:137
  291.8 0.8 multiply_subtract_fusion
  (86 shorter events, 7.4 us)
Async XLA Ops:
  7.2 272.9 %copy-start = (bf16[608,64]{0,1:T(8,128)(2,1)S(1)}, bf16[608,64]{0,1:T(8,128)(2,1)}, u32[]{:S(2)}) copy-start(bf16[608,64]{0,1:T(8,128)(2,1)} %param.20) | copy-start | bytes 233476
  7.2 141.9 %all-gather.7.cloned.1.call-start = ((), (), s32[]{:S(2)}) async-start(), calls=%async_computation.4 | async-start | bytes 3833856 | tf_op jit(solution)/shard_map/all_gather | solution.py:102
  15.9 11.8 %copy-start.3 = (f32[8,2,2432]{2,1,0:T(2,128)S(1)}, f32[8,2,2432]{2,1,0:T(2,128)}, u32[]{:S(2)}) copy-start(f32[8,2,2432]{2,1,0:T(2,128)} %param.16) | copy-start | bytes 466948
  37.4 5.4 %copy-start.5 = (f32[3,64]{1,0:T(4,128)S(1)}, f32[3,64]{1,0:T(4,128)}, u32[]{:S(2)}) copy-start(f32[3,64]{1,0:T(4,128)} %param.21) | copy-start | bytes 2308
  44.6 27.5 %copy-start.6 = (s32[8]{0:T(128)S(1)}, s32[8]{0:T(128)}, u32[]{:S(2)}) copy-start(s32[8]{0:T(128)} %param.22) | copy-start | bytes 100
  66.1 166.6 %all-gather.9.cloned.1.call-start = ((), (), s32[]{:S(2)}) async-start(), calls=%async_computation.5 | async-start | bytes 2662400 | tf_op jit(solution)/shard_map/all_gather | solution.py:77
  68.6 13.0 %all-to-all-start.1 = ((bf16[8,24,512]{2,1,0:T(8,128)(2,1)}), bf16[8,24,512]{2,1,0:T(8,128)(2,1)S(1)}, u32[]{:S(2)}, u32[]{:S(2)}) async-start(bf16[8,24,512]{2,1,0:T(8,128)(2,1)} %multiply_convert_fusion), calls=%async_computation.1 | async-start | bytes 393216 | tf_op jit(solution)/shard_map/all_to_all | solution.py:100
  190.9 12.9 %copy-start.1 = (bf16[1664,8,64]{2,1,0:T(8,128)(2,1)S(1)}, bf16[1664,8,64]{2,1,0:T(8,128)(2,1)}, u32[]{:S(2)}) copy-start(bf16[1664,8,64]{2,1,0:T(8,128)(2,1)} %reshape_squeeze.17) | copy-start | bytes 5111812
  209.4 26.1 %all-to-all-start.2 = ((bf16[8,24,512]{2,1,0:T(8,128)(2,1)}), bf16[8,24,512]{2,1,0:T(8,128)(2,1)S(1)}, u32[]{:S(2)}, u32[]{:S(2)}) async-start(bf16[8,24,512]{2,1,0:T(8,128)(2,1)} %reshape.176), calls=%async_computation.2 | async-start | bytes 393216 | tf_op jit(solution)/shard_map/all_to_all | solution.py:119
  217.1 55.8 %reduce-scatter.4.cloned.1.call-start = ((), (), s32[]{:S(2)}) async-start(), calls=%async_computation.6 | async-start | bytes 3112960
  235.5 3.2 %copy-start.7 = (s32[8]{0:T(128)S(1)}, s32[8]{0:T(128)}, u32[]{:S(2)}) copy-start(s32[8]{0:T(128)} %param.23) | copy-start | bytes 100
  237.7 36.4 %copy-start.2 = (bf16[8,24,608]{2,1,0:T(8,128)(2,1)S(1)}, bf16[8,24,608]{2,1,0:T(8,128)(2,1)}, u32[]{:S(2)}) copy-start(bf16[8,24,608]{2,1,0:T(8,128)(2,1)} %param.12) | copy-start | bytes 700420
  237.7 54.0 %copy-start.4 = (f32[8,24,64]{2,1,0:T(8,128)S(1)}, f32[8,24,64]{2,1,0:T(8,128)}, u32[]{:S(2)}) copy-start(f32[8,24,64]{2,1,0:T(8,128)} %param.14) | copy-start | bytes 147460
Sparse Core Ops, SparseCore 0:
  66.2 82.8 all-gather.6
  152.4 80.2 all-gather.8
  237.9 34.9 reduce-scatter.3
where the time goes:
time: 300 us; the launch traced here: 299 us
  waiting for transfers between devices  125 us (42%)
  blocking collectives  57 us (19%)
  local copies, waits for them, and re-layouts  50.3 us (17%)
  matrix products  21.3 us (7%)
  other arithmetic  19.7 us (7%)
  between operations  14.2 us (5%)
  starting transfers between devices  11.3 us (4%)
    all_gather x1, waiting for transfers between devices, per_device(): all_kv = lax.all_gather(group_kv, 'rm', axis=0, tiled=False)  66.5 us
    unnamed x4, waiting for transfers between devices  34.8 us
    slice x1, local copies, waits for them, and re-layouts, per_device(): values = all_kv[:, :, 1].reshape(key_count, heads_local, HD)  25.3 us
    all_to_all x1, blocking collectives, per_device(): group_kv = lax.all_to_all(kv_rows, 'rq', 0, 0, tiled=True)  21.4 us
    all_gather x2, blocking collectives, gather_features(): stacked = lax.all_gather(local, 'col', axis=0, tiled=False)  18.6 us
    all_gather x1, waiting for transfers between devices, per_device(): lax.all_gather(jnp.transpose(out_weight), ROW, axis=0, tiled=True)  15.6 us
    sub x1, other arithmetic, attend_one(): scores - top_score  12.9 us
    psum x1, blocking collectives, per_device(): lax.psum(jnp.dot(modulated.reshape(requests * patches, slab_width), final...  11.4 us
  transfers between devices with their start and end apart: 5, of which 4 were waited for; matrix products, arithmetic and copies ran while one was open for 23% of the time, Pallas kernels for 0%

commit v1 on v0

--- a/solution.py
+++ b/solution.py
@@ -74,7 +74,10 @@
     block_len = patches + text_rows
     groups = lax.axis_size("rq")
     members = lax.axis_size("rm")
-    weight_t = lax.all_gather(jnp.transpose(out_weight), ROW, axis=0, tiled=True)
+    weight_t = jnp.concatenate(
+        lax.all_to_all(jnp.stack([jnp.transpose(out_weight)] * lax.axis_size(ROW)), ROW, 0, 0),
+        axis=0,
+    )
     img_full = gather_features(img_hidden)
     txt_full = gather_features(txt_hidden)
     img_wide = img_full.astype(jnp.float32)

time: 300 us -> 342 us (1.14)
  waiting for transfers between devices: 125 us -> 146 us
  blocking collectives: 57 us -> 69.1 us
  starting transfers between devices: 11.3 us -> 18.7 us
    all_gather x1, waiting for transfers between devices: 66.5 us -> 109 us  [per_device(): all_kv = lax.all_gather(group_kv, 'rm', axis=0, tiled=False)]
    all_gather x1 -> x0, waiting for transfers between devices: 15.6 us -> none  [per_device(): lax.all_gather(jnp.transpose(out_weight), ROW, axis=0, tiled=True)]
    all_to_all x0 -> x1, blocking collectives: none -> 12.1 us  [per_device(): group_queries = lax.all_to_all(queries, 'rq', 0, 0, tiled=True)]
    all_to_all x1, starting transfers between devices: 3.57 us -> 12.8 us  [per_device(): lax.all_to_all(jnp.stack([jnp.transpose(out_weight)] * lax.axis_size(ROW)...]
    all_to_all x1, waiting for transfers between devices: 8.19 us -> 0.01 us  [per_device(): lax.all_to_all(jnp.stack([jnp.transpose(out_weight)] * lax.axis_size(ROW)...]
    all_to_all x1, waiting for transfers between devices: 0.01 us -> 6.89 us  [per_device(): lax.all_to_all(attended, 'rq', 0, 0, tiled=True)]
    unnamed x4 -> x3, waiting for transfers between devices: 34.8 us -> 29.9 us
  transfers between devices with their start and end apart: 5 -> 4, of which waited for: 4 -> 3; matrix products, arithmetic and copies ran while one was open for 23% -> 20% of each run, Pallas kernels for 0% -> 0%
where the time goes in v1:
time: 342 us; the launch traced here: 341 us
  waiting for transfers between devices  146 us (43%)
  blocking collectives  69.1 us (20%)
  local copies, waits for them, and re-layouts  52 us (15%)
  matrix products  21.3 us (6%)
  other arithmetic  18.9 us (6%)
  starting transfers between devices  18.7 us (5%)
  between operations  14.5 us (4%)
    all_gather x1, waiting for transfers between devices, per_device(): all_kv = lax.all_gather(group_kv, 'rm', axis=0, tiled=False)  109 us
    unnamed x3, waiting for transfers between devices  29.9 us
    slice x1, local copies, waits for them, and re-layouts, per_device(): values = all_kv[:, :, 1].reshape(key_count, heads_local, HD)  25.3 us
    all_to_all x1, blocking collectives, per_device(): group_kv = lax.all_to_all(kv_rows, 'rq', 0, 0, tiled=True)  21.4 us
    all_gather x2, blocking collectives, gather_features(): stacked = lax.all_gather(local, 'col', axis=0, tiled=False)  18.6 us
    sub x1, other arithmetic, attend_one(): scores - top_score  12.8 us
    all_to_all x1, starting transfers between devices, per_device(): lax.all_to_all(jnp.stack([jnp.transpose(out_weight)] * lax.axis_size(ROW)...  12.8 us
    all_to_all x1, blocking collectives, per_device(): group_queries = lax.all_to_all(queries, 'rq', 0, 0, tiled=True)  12.1 us
  transfers between devices with their start and end apart: 4, of which 3 were waited for; matrix products, arithmetic and copies ran while one was open for 20% of the time, Pallas kernels for 0%

profile of v1, /device:TPU:1, one launch (start us, length us, event | category | flops | bytes accessed | tf_op | source)
XLA Modules:
  0.0 340.6 jit_solution(3948090975154213054)
XLA Ops:
  7.2 8.6 %all-gather.1 = bf16[32,2,608]{2,1,0:T(2,128)(2,1)S(1)} all-gather(bf16[8,2,608]{2,1,0:T(2,128)(2,1)} %param.13), channel_id=3, replica_groups=mesh['rq'=8,'rm'=8,'col'=4] {'col'}, dimensions={0}, use_global_device_ids=true | all-gather | bytes 97280 | tf_op jit(solution)/shard_map/all_gather | solution.py:35
  16.1 10.0 %all-gather = bf16[32,24,608]{2,1,0:T(8,128)(2,1)S(1)} all-gather(bf16[8,24,608]{2,1,0:T(8,128)(2,1)} %param.12), channel_id=2, replica_groups=mesh['rq'=8,'rm'=8,'col'=4] {'col'}, dimensions={0}, use_global_device_ids=true | all-gather | bytes 1167360 | tf_op jit(solution)/shard_map/all_gather | solution.py:35
  27.9 3.2 fusion.28
  31.2 2.6 copy.80
  33.8 2.2 reshape.187
  36.0 0.9 add_bitcast_fusion
  37.5 4.8 %convolution_bitcast_fusion.1 = f32[3,192,512]{2,1,0:T(8,128)S(1)} fusion(bf16[3,2432,512]{2,1,0:T(8,128)(2,1)} %param.17, bf16[192,2432]{1,0:T(8,128)(2,1)S(1)} %fusion.12), kind=kOutput, calls=%fused_computation.22 | convolution fusion | flops 1434451968 | bytes 9584640 | tf_op jit(solution)/shard_map/td,cde->cte/dot_general | solution.py:88
  44.6 21.4 %all_to_all.20 = bf16[8,2,26,512]{3,1,2,0:T(2,128)(2,1)} all-to-all(bf16[8,2,26,512]{3,1,2,0:T(2,128)(2,1)S(1)} %copy.93), channel_id=1, replica_groups=mesh['rq'=8,'rm'=8,'col'=4] {'rq'}, dimensions={0} | all-to-all | bytes 851968 | tf_op jit(solution)/shard_map/all_to_all | solution.py:104
  67.1 12.1 %all_to_all.21 = bf16[8,24,512]{2,1,0:T(8,128)(2,1)S(1)} all-to-all(bf16[8,24,512]{2,1,0:T(8,128)(2,1)S(1)} %multiply_convert_fusion), channel_id=1, replica_groups=mesh['rq'=8,'rm'=8,'col'=4] {'rq'}, dimensions={0} | all-to-all | bytes 393216 | tf_op jit(solution)/shard_map/all_to_all | solution.py:103
  79.3 1.7 stack.11
  80.9 12.8 %all-to-all-start.3 = ((bf16[64,38,512]{2,1,0:T(8,128)(2,1)}), bf16[64,38,512]{2,1,0:T(8,128)(2,1)}, u32[]{:S(2)}, u32[]{:S(2)}) async-start(bf16[64,38,512]{2,1,0:T(8,128)(2,1)} %stack.11), calls=%async_computation.3 | async-start | bytes 5242880 | tf_op jit(solution)/shard_map/all_to_all | solution.py:78
  93.8 0.6 dynamic_slice.8
  94.4 0.7 fusion.60
  95.0 1.0 reshape.180
  96.0 109.2 %all-gather.5.cloned.1.call-done = bf16[64,2,26,512]{3,1,2,0:T(2,128)(2,1)} async-done(((bf16[8,2,26,512]{3,1,2,0:T(2,128)(2,1)}), bf16[64,2,26,512]{3,1,2,0:T(2,128)(2,1)}) %all-gather.5.cloned.1.call-update) | async-done | bytes 3407888 | tf_op jit(solution)/shard_map/all_gather | solution.py:105
  205.3 25.3 %slice_reduce_fusion.1 = (bf16[8,8,26,512]{3,2,1,0:T(8,128)(2,1)}, bf16[8,8,26,512]{3,2,1,0:T(8,128)(2,1)}) fusion(bf16[8,8,2,26,512]{4,2,3,1,0:T(2,128)(2,1)} %bitcast.116), kind=kLoop, calls=%fused_computation.13 | loop fusion | bytes 6815744 | tf_op jit(solution)/shard_map/slice | solution.py:108
  230.6 4.3 %reshape_squeeze.19 = bf16[1664,8,64]{2,1,0:T(8,128)(2,1)S(1)} reshape(bf16[8,8,26,512]{3,2,1,0:T(8,128)(2,1)} %get-tuple-element.3) | data formatting | bytes 3407872 | tf_op jit(solution)/shard_map/reshape;squeeze | solution.py:107
  234.9 5.7 %reshape_squeeze.17 = bf16[1664,8,64]{2,1,0:T(8,128)(2,1)} reshape(bf16[8,8,26,512]{3,2,1,0:T(8,128)(2,1)} %get-tuple-element.2) | data formatting | bytes 3407872 | tf_op jit(solution)/shard_map/reshape;squeeze | solution.py:108
  240.6 6.4 %fusion.10 = f32[8,192,1664]{2,1,0:T(8,128)} fusion(bf16[1664,8,64]{2,1,0:T(8,128)(2,1)S(1)} %reshape_squeeze.19, bf16[192,8,64]{2,1,0:T(8,128)(2,1)} %reshape.180), kind=kOutput, calls=%fused_computation.15 | convolution fusion | flops 327155712 | bytes 12124160 | tf_op jit(solution)/shard_map/qhd,khd->hqk/dot_general | solution.py:42
  247.0 12.8 %fusion.67 = (f32[8,192]{1,0:T(8,128)S(1)}, bf16[8,192,1664]{2,1,0:T(8,128)(2,1)}) fusion(f32[8,192,1664]{2,1,0:T(8,128)} %fusion.10, pred[1664]{0:T(1024)(128)(4,1)S(1)} %fusion.60), kind=kOutput, calls=%fused_computation.113 | output fusion | flops 20448896 | bytes 15343232 | tf_op jit(solution)/shard_map/sub | solution.py:47
  259.8 4.4 %fusion.23 = bf16[192,8,64]{0,2,1:T(8,128)(2,1)S(1)} fusion(bf16[8,192,1664]{2,1,0:T(8,128)(2,1)} %get-tuple-element.29, bf16[1664,8,64]{2,1,0:T(8,128)(2,1)S(1)} %copy-done.1, f32[192,8]{0,1:T(8,128)S(1)} %bitcast.130), kind=kOutput, calls=%fused_computation.25 | convolution fusion | flops 327352320 | bytes 7018496 | tf_op jit(solution)/shard_map/hqk,khd->qhd/dot_general | solution.py:49
  264.5 0.9 reshape.181
  265.4 5.8 %all-to-all-start.2 = ((bf16[8,24,512]{2,1,0:T(8,128)(2,1)}), bf16[8,24,512]{2,1,0:T(8,128)(2,1)S(1)}, u32[]{:S(2)}, u32[]{:S(2)}) async-start(bf16[8,24,512]{2,1,0:T(8,128)(2,1)} %reshape.181), calls=%async_computation.2 | async-start | bytes 393216 | tf_op jit(solution)/shard_map/all_to_all | solution.py:122
  271.3 2.8 reshape.183
  274.1 6.9 %all-to-all-done.2 = bf16[8,24,512]{2,1,0:T(8,128)(2,1)S(1)} async-done(((bf16[8,24,512]{2,1,0:T(8,128)(2,1)}), bf16[8,24,512]{2,1,0:T(8,128)(2,1)S(1)}, u32[]{:S(2)}, u32[]{:S(2)}) %all-to-all-start.2) | async-done | bytes 196640 | tf_op jit(solution)/shard_map/all_to_all | solution.py:122
  281.0 2.3 convolution_bitcast_fusion
  283.3 0.9 dynamic-slice_bitcast_fusion.1
  284.3 29.9 %reduce-scatter.4.cloned.1.call-done = f32[608,192]{1,0:T(8,128)} async-done(((f32[2432,192]{1,0:T(8,128)}), f32[608,192]{1,0:T(8,128)}) %reduce-scatter.4.cloned.1.call-update) | async-done | bytes 466960
  314.1 1.3 copy.106
  315.6 5.5 %all-reduce = (f32[8,24]{1,0:T(8,128)S(1)}, f32[8,24]{1,0:T(8,128)S(1)}) all-reduce(f32[8,24]{1,0:T(8,128)S(1)} %get-tuple-element.5, f32[8,24]{1,0:T(8,128)S(1)} %get-tuple-element.4), channel_id=1, replica_groups=mesh['rq'=8,'rm'=8,'col'=4] {'col'}, use_global_device_ids=true, to_apply=%region_13.14 | all-reduce | flops 384 | bytes 3072 | tf_op jit(solution)/shard_map/psum | solution.py:135
  321.5 11.5 %psum.23 = f32[8,24,64]{2,1,0:T(8,128)S(1)} all-reduce(f32[8,24,64]{2,1,0:T(8,128)S(1)} %bitcast.128), channel_id=1, replica_groups=mesh['rq'=8,'rm'=8,'col'=4] {'col'}, use_global_device_ids=true, to_apply=%region_14.15 | all-reduce | flops 12288 | bytes 98304 | tf_op jit(solution)/shard_map/psum | solution.py:140
  333.0 0.8 multiply_subtract_fusion
  (87 shorter events, 6.8 us)
Async XLA Ops:
  7.2 314.2 %copy-start = (bf16[608,64]{0,1:T(8,128)(2,1)S(1)}, bf16[608,64]{0,1:T(8,128)(2,1)}, u32[]{:S(2)}) copy-start(bf16[608,64]{0,1:T(8,128)(2,1)} %param.20) | copy-start | bytes 233476
  7.2 198.1 %all-gather.5.cloned.1.call-start = ((), (), s32[]{:S(2)}) async-start(), calls=%async_computation.5 | async-start | bytes 3833856 | tf_op jit(solution)/shard_map/all_gather | solution.py:105
  15.9 11.8 %copy-start.3 = (f32[8,2,2432]{2,1,0:T(2,128)S(1)}, f32[8,2,2432]{2,1,0:T(2,128)}, u32[]{:S(2)}) copy-start(f32[8,2,2432]{2,1,0:T(2,128)} %param.16) | copy-start | bytes 466948
  37.4 5.4 %copy-start.6 = (f32[3,64]{1,0:T(4,128)S(1)}, f32[3,64]{1,0:T(4,128)}, u32[]{:S(2)}) copy-start(f32[3,64]{1,0:T(4,128)} %param.21) | copy-start | bytes 2308
  44.2 35.1 %copy-start.5 = (bf16[512,38]{0,1:T(8,128)(2,1)S(1)}, bf16[512,38]{0,1:T(8,128)(2,1)}, u32[]{:S(2)}) copy-start(bf16[512,38]{0,1:T(8,128)(2,1)} %param.19) | copy-start | bytes 116740
  79.3 14.5 %copy-start.7 = (s32[8]{0:T(128)S(1)}, s32[8]{0:T(128)}, u32[]{:S(2)}) copy-start(s32[8]{0:T(128)} %param.22) | copy-start | bytes 100
  80.9 184.5 %all-to-all-start.3 = ((bf16[64,38,512]{2,1,0:T(8,128)(2,1)}), bf16[64,38,512]{2,1,0:T(8,128)(2,1)}, u32[]{:S(2)}, u32[]{:S(2)}) async-start(bf16[64,38,512]{2,1,0:T(8,128)(2,1)} %stack.11), calls=%async_computation.3 | async-start | bytes 5242880 | tf_op jit(solution)/shard_map/all_to_all | solution.py:78
  247.0 12.8 %copy-start.1 = (bf16[1664,8,64]{2,1,0:T(8,128)(2,1)S(1)}, bf16[1664,8,64]{2,1,0:T(8,128)(2,1)}, u32[]{:S(2)}) copy-start(bf16[1664,8,64]{2,1,0:T(8,128)(2,1)} %reshape_squeeze.17) | copy-start | bytes 5111812
  265.4 15.6 %all-to-all-start.2 = ((bf16[8,24,512]{2,1,0:T(8,128)(2,1)}), bf16[8,24,512]{2,1,0:T(8,128)(2,1)S(1)}, u32[]{:S(2)}, u32[]{:S(2)}) async-start(bf16[8,24,512]{2,1,0:T(8,128)(2,1)} %reshape.181), calls=%async_computation.2 | async-start | bytes 393216 | tf_op jit(solution)/shard_map/all_to_all | solution.py:122
  271.3 42.8 %reduce-scatter.4.cloned.1.call-start = ((), (), s32[]{:S(2)}) async-start(), calls=%async_computation.6 | async-start | bytes 3112960
  281.0 3.2 copy-start.8
  283.3 32.1 %copy-start.2 = (bf16[8,24,608]{2,1,0:T(8,128)(2,1)S(1)}, bf16[8,24,608]{2,1,0:T(8,128)(2,1)}, u32[]{:S(2)}) copy-start(bf16[8,24,608]{2,1,0:T(8,128)(2,1)} %param.12) | copy-start | bytes 700420
  283.3 49.7 %copy-start.4 = (f32[8,24,64]{2,1,0:T(8,128)S(1)}, f32[8,24,64]{2,1,0:T(8,128)}, u32[]{:S(2)}) copy-start(f32[8,24,64]{2,1,0:T(8,128)} %param.14) | copy-start | bytes 147460
Sparse Core Ops, SparseCore 0:
  66.2 139.0 all-gather.4
  283.4 30.6 reduce-scatter.3
